TPU v7x, 256 devices: a whole 4x4x8 slice. The times are simulated.
256 devices in a mesh: tm: 64 (over z, x, core), wafer: 4 (over y).
Axes of the slice: x: 4, y: 4, z: 8, core: 2. Of those that a mesh axis runs over, the one named last changes fastest.
Arguments:
- timestream: bfloat16 [1024, 262144], P('wafer', 'tm'), may hold values from -6 to 6
- sample_weight: bfloat16 [1024, 262144], P('wafer', 'tm'), may hold values from 0 to 4
- response: float32 [3, 1024], replicated, may hold values from -1 to 1
- band_filter: bfloat16 [256, 256], replicated, may hold values from -0.375 to 0.375
- whiten: bfloat16 [7, 1024, 1024], P(None, ('tm', 'wafer')), as said below
- group_wafer: int32 [64], replicated, may hold values from 0 to 6
- pointing: bfloat16 [1024, 6, 256, 256], P(('tm', 'wafer')), may hold values from -0.15625 to 0.15625
- tile_list: int32 [1024, 6], P(('tm', 'wafer')), may hold values from 0 to 2047, as said below
- tile_home: int32 [2048], replicated, may hold values from 0 to 2047, as said below
- solution: float32 [2048, 3, 256], P('tm'), may hold values from -6 to 6
- direction: float32 [2048, 3, 256], P('tm'), may hold values from -6 to 6
- cg_scalars: float32 [2], replicated, may hold values from 0.5 to 1.5
Outputs:
- solution_next: float32 [2048, 3, 256], P('tm')
- residual_next: float32 [2048, 3, 256], P('tm')
- direction_next: float32 [2048, 3, 256], P('tm')
Inputs may be any that keep to these rules, and one draw needn't show every extreme that they name: `tile_list`: the tiles named in the spans of one device (one index of tm and one of wafer) are all different; among them at most 2 have their row tile_home on one index of tm, and in every draw, for each index of wafer, some index of tm owns exactly 2 tiles named by every device of that wafer index. A permutation: row tile_home[i] of a map holds sky tile i. `whiten`: each whitening matrix is symmetric.
All inputs are finite; a program needn't handle non-finite values.
Results may differ from a plain program's by a relative error of at most 0.0033.
The roundings to bfloat16 on the way count: a program that leaves them out, or rounds other values in their place, can miss the bound.
Values may be sent and summed in bfloat16 or wider, within the bound.
No kernel may reach another device: no remote copies, remote signals or barrier semaphores. Data moves between devices by JAX's collectives and lax.ppermute only.
A program may use at most 128 MiB of HBM per device.

v0:
```python
import jax
import jax.numpy as jnp
from jax import lax
from jax.sharding import PartitionSpec as P


def shards(
    timestream,
    sample_weight,
    response,
    band_filter,
    whiten,
    group_wafer,
    pointing,
    tile_list,
    tile_home,
    solution,
    direction,
    cg_scalars,
):
    precise_mode = lax.Precision.HIGHEST
    tm_count = lax.axis_size("tm")
    tm_index = lax.axis_index("tm")
    step_size = cg_scalars[0]
    blend_weight = cg_scalars[1]
    updated = solution + step_size * direction
    short_map = updated.astype(jnp.bfloat16)
    tiles_own, comp_count, pixel_count = solution.shape
    spans_here, per_span = tile_list.shape
    samples = band_filter.shape[0]
    det_total = whiten.shape[2]
    row_count = spans_here * per_span
    capacity = max(2, (row_count + tm_count - 1) // tm_count)
    tile_ids = tile_list.reshape(row_count)
    home_rows = jnp.take(tile_home, tile_ids, axis=0)
    owners = home_rows // tiles_own
    local_slot = home_rows % tiles_own
    positions = jnp.arange(row_count, dtype=jnp.int32)
    earlier = (owners[:, None] == owners[None, :]) & (positions[None, :] < positions[:, None])
    before_count = jnp.sum(earlier.astype(jnp.int32), axis=1)
    targets = owners * capacity + before_count
    placing = targets[:, None] == jnp.arange(tm_count * capacity, dtype=jnp.int32)[None, :]
    requests = jnp.sum(jnp.where(placing, local_slot[:, None], 0), axis=0)
    requests = requests.reshape(tm_count, capacity)
    asked_slots = lax.all_to_all(requests, "tm", split_axis=0, concat_axis=0, tiled=True)
    served = jnp.take(short_map, asked_slots, axis=0)
    replies, asked_slots = (
        lax.all_to_all(served, "tm", split_axis=0, concat_axis=0, tiled=True),
        asked_slots,
    )
    fetched = jnp.take(
        replies.reshape(tm_count * capacity, comp_count, pixel_count), targets, axis=0
    )
    fetched = fetched.reshape(spans_here, per_span, comp_count, pixel_count)
    signal_parts = jnp.einsum(
        "cktp,ckjp->cjt", pointing, fetched, preferred_element_type=jnp.float32
    )
    wafer_pick = group_wafer[tm_index]
    matrix = lax.dynamic_index_in_dim(
        lax.all_gather(whiten, ("tm", "wafer"), axis=1, tiled=True), wafer_pick, 0, keepdims=False
    )
    columns, column_weights = (
        lax.all_to_all(timestream, "wafer", split_axis=1, concat_axis=0, tiled=True),
        lax.all_to_all(sample_weight, "wafer", split_axis=1, concat_axis=0, tiled=True),
    )
    column_weights = column_weights.astype(jnp.float32).reshape(det_total, spans_here, samples)
    signal = jnp.einsum("jd,cjt->dct", response, signal_parts, precision=precise_mode)
    errors = (
        (columns.astype(jnp.float32).reshape(det_total, spans_here, samples) - signal)
        * column_weights
    ).astype(jnp.bfloat16)
    filtered = jnp.dot(
        errors.reshape(det_total * spans_here, samples),
        band_filter,
        preferred_element_type=jnp.float32,
    )
    filtered = filtered.astype(jnp.bfloat16).reshape(det_total, spans_here * samples)
    whitened = jnp.dot(matrix, filtered, preferred_element_type=jnp.float32).astype(jnp.bfloat16)
    smoothed = lax.dot_general(
        whitened.reshape(det_total * spans_here, samples),
        band_filter,
        (((1,), (1,)), ((), ())),
        preferred_element_type=jnp.float32,
    )
    smoothed = smoothed.astype(jnp.bfloat16).reshape(det_total, spans_here, samples)
    stokes = jnp.einsum(
        "jd,dct->cjt",
        response,
        smoothed.astype(jnp.float32) * column_weights,
        precision=precise_mode,
    )
    stokes_short = stokes.astype(jnp.bfloat16)
    partial_value = jnp.einsum(
        "cjt,cktp->ckjp", stokes_short, pointing, preferred_element_type=jnp.float32
    )
    partial_value = partial_value.reshape(row_count, comp_count * pixel_count)
    outgoing = jnp.dot(placing.astype(jnp.float32).T, partial_value, precision=precise_mode)
    outgoing = outgoing.reshape(tm_count, capacity, comp_count, pixel_count)
    arrived = lax.all_to_all(outgoing, "tm", split_axis=0, concat_axis=0, tiled=True)
    slot_hits = (
        asked_slots.reshape(-1)[None, :] == jnp.arange(tiles_own, dtype=jnp.int32)[:, None]
    ).astype(jnp.float32)
    owned_sum = jnp.dot(
        slot_hits,
        arrived.reshape(tm_count * capacity, comp_count * pixel_count),
        precision=precise_mode,
    )
    owned_sum = owned_sum.reshape(tiles_own, comp_count, pixel_count)
    summed = lax.psum(owned_sum, "wafer")
    residual_next = summed * float(det_total) ** (-0.5)
    direction_next = residual_next + blend_weight * direction
    return (updated, residual_next, direction_next)


def solution(mesh):
    in_specs = (
        P("wafer", "tm"),
        P("wafer", "tm"),
        P(),
        P(),
        P(None, ("tm", "wafer"), None),
        P(),
        P(("tm", "wafer"), None, None, None),
        P(("tm", "wafer"), None),
        P(),
        P("tm", None, None),
        P("tm", None, None),
        P(),
    )
    out_specs = (P("tm", None, None), P("tm", None, None), P("tm", None, None))
    return jax.shard_map(shards, mesh=mesh, in_specs=in_specs, out_specs=out_specs, check_vma=False)
```

profile of v0, /device:TPU:2, one launch (start us, length us, event | category | flops | bytes accessed | tf_op | source)
XLA Modules:
  0.0 281.9 jit_solution(5731134282750877064)
XLA Ops:
  12.9 12.0 %all-to-all-start = ((s32[64,1,2]{2,1,0:T(1,128)}), s32[64,1,2]{2,1,0:T(1,128)S(1)}, u32[]{:S(2)}, u32[]{:S(2)}) async-start(s32[64,1,2]{2,1,0:T(1,128)} %bitcast.2), calls=%async_computation | async-start | bytes 65536 | tf_op jit(solution)/shard_map/all_to_all | solution.py:45
  28.7 4.8 %all-to-all-done = s32[64,1,2]{2,1,0:T(1,128)S(1)} async-done(((s32[64,1,2]{2,1,0:T(1,128)}), s32[64,1,2]{2,1,0:T(1,128)S(1)}, u32[]{:S(2)}, u32[]{:S(2)}) %all-to-all-start) | async-done | bytes 544 | tf_op jit(solution)/shard_map/all_to_all | solution.py:45
  35.9 5.5 %all-to-all-start.2 = ((bf16[64,2,3,256]{3,1,2,0:T(2,128)(2,1)}), bf16[64,2,3,256]{3,1,2,0:T(2,128)(2,1)S(1)}, u32[]{:S(2)}, u32[]{:S(2)}) async-start(bf16[64,2,3,256]{3,1,2,0:T(2,128)(2,1)} %broadcast_select_fusion), calls=%async_computation.2 | async-start | bytes 393216 | tf_op jit(solution)/shard_map/all_to_all | solution.py:48
  45.5 7.3 %all-to-all-done.2 = bf16[64,2,3,256]{3,1,2,0:T(2,128)(2,1)S(1)} async-done(((bf16[64,2,3,256]{3,1,2,0:T(2,128)(2,1)}), bf16[64,2,3,256]{3,1,2,0:T(2,128)(2,1)S(1)}, u32[]{:S(2)}, u32[]{:S(2)}) %all-to-all-start.2) | async-done | bytes 196640 | tf_op jit(solution)/shard_map/all_to_all | solution.py:48
  52.7 4.5 %all-to-all-start.1 = ((bf16[256,4,1024]{0,2,1:T(8,128)(2,1)}), bf16[256,4,1024]{0,2,1:T(8,128)(2,1)}, u32[]{:S(2)}, u32[]{:S(2)}) async-start(bf16[256,4,1024]{0,2,1:T(8,128)(2,1)} %bitcast.99), calls=%async_computation.1 | async-start | bytes 4194304 | tf_op jit(solution)/shard_map/all_to_all | solution.py:63
  61.3 25.7 %all-to-all-done.1 = bf16[256,4,1024]{0,2,1:T(8,128)(2,1)} async-done(((bf16[256,4,1024]{0,2,1:T(8,128)(2,1)}), bf16[256,4,1024]{0,2,1:T(8,128)(2,1)}, u32[]{:S(2)}, u32[]{:S(2)}) %all-to-all-start.1) | async-done | bytes 2097184 | tf_op jit(solution)/shard_map/all_to_all | solution.py:63
  87.1 4.6 %all-to-all-start.3 = ((bf16[256,4,1024]{0,2,1:T(8,128)(2,1)}), bf16[256,4,1024]{0,2,1:T(8,128)(2,1)}, u32[]{:S(2)}, u32[]{:S(2)}) async-start(bf16[256,4,1024]{0,2,1:T(8,128)(2,1)} %bitcast.98), calls=%async_computation.3 | async-start | bytes 4194304 | tf_op jit(solution)/shard_map/all_to_all | solution.py:64
  99.8 4.8 %copy.114 = f32[4,256,1024]{1,0,2:T(4,128)} copy(f32[4,256,1024]{1,2,0:T(8,128)S(1)} %convert_bitcast_fusion.1) | data formatting | bytes 8388608 | tf_op jit(solution)/shard_map/convert_element_type | solution.py:69
  104.7 5.8 %reshape.326 = f32[1024,4,256]{0,2,1:T(8,128)} reshape(f32[4,256,1024]{1,0,2:T(4,128)} %copy.114) | data formatting | bytes 8388608 | tf_op jit(solution)/shard_map/convert_element_type | solution.py:69
  110.5 20.1 %all-to-all-done.3 = bf16[256,4,1024]{0,2,1:T(8,128)(2,1)} async-done(((bf16[256,4,1024]{0,2,1:T(8,128)(2,1)}), bf16[256,4,1024]{0,2,1:T(8,128)(2,1)}, u32[]{:S(2)}, u32[]{:S(2)}) %all-to-all-start.3) | async-done | bytes 2097184 | tf_op jit(solution)/shard_map/all_to_all | solution.py:64
  132.8 4.7 %copy.124 = f32[4,256,1024]{1,0,2:T(4,128)} copy(f32[4,256,1024]{1,2,0:T(8,128)S(1)} %convert_bitcast_fusion) | data formatting | bytes 8388608 | tf_op jit(solution)/shard_map/convert_element_type | solution.py:66
  137.4 5.9 %reshape.327 = f32[1024,4,256]{0,2,1:T(8,128)} reshape(f32[4,256,1024]{1,0,2:T(4,128)} %copy.124) | data formatting | bytes 8388608 | tf_op jit(solution)/shard_map/convert_element_type | solution.py:66
  143.3 7.2 %fusion.2 = bf16[1024,4,256]{0,2,1:T(8,128)(2,1)} fusion(f32[1024,4,256]{0,2,1:T(8,128)} %reshape.327, f32[1024,4,256]{0,2,1:T(8,128)} %reshape.326, f32[4,3,256]{2,1,0:T(4,128)S(1)} %convolution_bitcast_fusion, f32[3,1024]{1,0:T(4,128)S(1)} %copy-done.4), kind=kOutput, calls=%fused_computation.8 | convolution fusion | flops 40894464 | bytes 10510336 | tf_op jit(solution)/shard_map/jd,cjt->dct/dot_general | solution.py:67
  150.5 4.3 %copy.125 = bf16[1024,4,256]{2,1,0:T(4,128)(2,1)} copy(bf16[1024,4,256]{0,2,1:T(8,128)(2,1)} %fusion.2) | data formatting | bytes 4194304 | tf_op jit(solution)/shard_map/convert_element_type | solution.py:71
  162.5 4.4 %reshape.322 = bf16[1024,1024]{1,0:T(8,128)(2,1)} reshape(bf16[4096,256]{1,0:T(8,128)(2,1)} %convolution_convert_fusion.1) | data formatting | bytes 4194304 | tf_op jit(solution)/shard_map/reshape | solution.py:77
  166.9 7.8 %constant_dynamic-slice_fusion = bf16[1,1024,1024]{2,0,1:T(2,128)(2,1)S(1)} fusion(bf16[7,1024,1024]{2,0,1:T(8,128)(2,1)} %all-gather.2.cloned.1.call-done, s32[]{:T(128)S(6)} %select_n.167), kind=kLoop, calls=%fused_computation.81 | loop fusion | bytes 4194308 | tf_op jit(solution)/shard_map/jit(dynamic_index_in_dim)/dynamic_slice | solution.py:59
  178.4 4.4 %reshape.323 = bf16[4096,256]{1,0:T(8,128)(2,1)} reshape(bf16[1024,1024]{1,0:T(8,128)(2,1)} %fusion.6) | data formatting | bytes 4194304 | tf_op jit(solution)/shard_map/reshape | solution.py:80
  182.8 4.3 %fusion = f32[4096,256]{1,0:T(8,128)} fusion(bf16[4096,256]{1,0:T(8,128)(2,1)} %reshape.323, bf16[256,256]{1,0:T(8,128)(2,1)S(1)} %copy-done.2), kind=kOutput, calls=%fused_computation.4 | convolution fusion | flops 538968064 | bytes 6422528 | tf_op jit(solution)/shard_map/dot_general | solution.py:79
  187.1 5.2 %reshape.328 = f32[1024,4,256]{2,1,0:T(4,128)} reshape(f32[4096,256]{1,0:T(8,128)} %fusion) | data formatting | bytes 8388608 | tf_op jit(solution)/shard_map/convert_element_type | solution.py:89
  192.3 5.2 %copy.126 = f32[1024,4,256]{0,2,1:T(8,128)} copy(f32[1024,4,256]{2,1,0:T(4,128)} %reshape.328) | data formatting | bytes 8388608 | tf_op jit(solution)/shard_map/convert_element_type | solution.py:89
  197.5 7.2 %fusion.10 = bf16[4,256,3,1]{1,2,3,0:T(4,128)(2,1)S(1)} fusion(f32[1024,4,256]{0,2,1:T(8,128)} %copy.126, f32[1024,4,256]{0,2,1:T(8,128)} %reshape.327, f32[3,1024]{1,0:T(4,128)S(1)} %copy-done.4), kind=kOutput, calls=%fused_computation.18 | convolution fusion | flops 38800384 | bytes 8407040 | tf_op jit(solution)/shard_map/jd,dct->cjt/dot_general | solution.py:86
  206.7 6.5 %all-to-all-start.4 = ((f32[64,2,3,256]{3,1,2,0:T(2,128)}), f32[64,2,3,256]{3,1,2,0:T(2,128)S(1)}, u32[]{:S(2)}, u32[]{:S(2)}) async-start(f32[64,2,3,256]{3,1,2,0:T(2,128)} %copy.129), calls=%async_computation.4 | async-start | bytes 786432 | tf_op jit(solution)/shard_map/all_to_all | solution.py:99
  216.7 11.3 %all-to-all-done.4 = f32[64,2,3,256]{3,1,2,0:T(2,128)S(1)} async-done(((f32[64,2,3,256]{3,1,2,0:T(2,128)}), f32[64,2,3,256]{3,1,2,0:T(2,128)S(1)}, u32[]{:S(2)}, u32[]{:S(2)}) %all-to-all-start.4) | async-done | bytes 393248 | tf_op jit(solution)/shard_map/all_to_all | solution.py:99
  232.7 40.0 %all-reduce.2.cloned.1.call-done = f32[32,3,256]{2,0,1:T(8,128)} async-done(((f32[32,3,256]{2,0,1:T(8,128)}), f32[32,3,256]{2,0,1:T(8,128)}) %all-reduce.2.cloned.1.call-update) | async-done | bytes 98320 | tf_op jit(solution)/shard_map/psum | solution.py:109
  (71 shorter events, 52.3 us)
Async XLA Ops:
  7.2 89.8 %copy-start = (bf16[4,6,256,256]{3,2,1,0:T(8,128)(2,1)S(1)}, bf16[4,6,256,256]{3,2,1,0:T(8,128)(2,1)}, u32[]{:S(2)}) copy-start(bf16[4,6,256,256]{3,2,1,0:T(8,128)(2,1)} %param.18) | copy-start | bytes 9437188
  7.2 159.8 %all-gather.2.cloned.1.call-start = ((), (), s32[]{:S(2)}) async-start(), calls=%async_computation.5 | async-start | bytes 16842752 | tf_op jit(solution)/shard_map/all_gather | solution.py:60
  12.9 20.6 %all-to-all-start = ((s32[64,1,2]{2,1,0:T(1,128)}), s32[64,1,2]{2,1,0:T(1,128)S(1)}, u32[]{:S(2)}, u32[]{:S(2)}) async-start(s32[64,1,2]{2,1,0:T(1,128)} %bitcast.2), calls=%async_computation | async-start | bytes 65536 | tf_op jit(solution)/shard_map/all_to_all | solution.py:45
  33.5 0.6 copy-start.3
  35.9 16.9 %all-to-all-start.2 = ((bf16[64,2,3,256]{3,1,2,0:T(2,128)(2,1)}), bf16[64,2,3,256]{3,1,2,0:T(2,128)(2,1)S(1)}, u32[]{:S(2)}, u32[]{:S(2)}) async-start(bf16[64,2,3,256]{3,1,2,0:T(2,128)(2,1)} %broadcast_select_fusion), calls=%async_computation.2 | async-start | bytes 393216 | tf_op jit(solution)/shard_map/all_to_all | solution.py:48
  52.7 34.3 %all-to-all-start.1 = ((bf16[256,4,1024]{0,2,1:T(8,128)(2,1)}), bf16[256,4,1024]{0,2,1:T(8,128)(2,1)}, u32[]{:S(2)}, u32[]{:S(2)}) async-start(bf16[256,4,1024]{0,2,1:T(8,128)(2,1)} %bitcast.99), calls=%async_computation.1 | async-start | bytes 4194304 | tf_op jit(solution)/shard_map/all_to_all | solution.py:63
  61.3 30.6 %copy-start.6 = (s32[64]{0:T(128)S(1)}, s32[64]{0:T(128)}, u32[]{:S(2)}) copy-start(s32[64]{0:T(128)} %param.17) | copy-start | bytes 772
  61.3 33.1 %copy-start.5 = (s32[4,6]{1,0:T(4,128)S(1)}, s32[4,6]{1,0:T(4,128)}, u32[]{:S(2)}) copy-start(s32[4,6]{1,0:T(4,128)} %param.19) | copy-start | bytes 292
  87.1 43.5 %all-to-all-start.3 = ((bf16[256,4,1024]{0,2,1:T(8,128)(2,1)}), bf16[256,4,1024]{0,2,1:T(8,128)(2,1)}, u32[]{:S(2)}, u32[]{:S(2)}) async-start(bf16[256,4,1024]{0,2,1:T(8,128)(2,1)} %bitcast.98), calls=%async_computation.3 | async-start | bytes 4194304 | tf_op jit(solution)/shard_map/all_to_all | solution.py:64
  137.4 5.9 %copy-start.4 = (f32[3,1024]{1,0:T(4,128)S(1)}, f32[3,1024]{1,0:T(4,128)}, u32[]{:S(2)}) copy-start(f32[3,1024]{1,0:T(4,128)} %param.14) | copy-start | bytes 36868
  154.8 4.1 %copy-start.2 = (bf16[256,256]{1,0:T(8,128)(2,1)S(1)}, bf16[256,256]{1,0:T(8,128)(2,1)}, u32[]{:S(2)}) copy-start(bf16[256,256]{1,0:T(8,128)(2,1)} %param.15) | copy-start | bytes 393220
  166.9 7.8 %copy-start.1 = (bf16[1024,1024]{1,0:T(8,128)(2,1)S(1)}, bf16[1024,1024]{1,0:T(8,128)(2,1)}, u32[]{:S(2)}) copy-start(bf16[1024,1024]{1,0:T(8,128)(2,1)} %reshape.322) | copy-start | bytes 6291460
  206.7 21.3 %all-to-all-start.4 = ((f32[64,2,3,256]{3,1,2,0:T(2,128)}), f32[64,2,3,256]{3,1,2,0:T(2,128)S(1)}, u32[]{:S(2)}, u32[]{:S(2)}) async-start(f32[64,2,3,256]{3,1,2,0:T(2,128)} %copy.129), calls=%async_computation.4 | async-start | bytes 786432 | tf_op jit(solution)/shard_map/all_to_all | solution.py:99
  213.2 59.5 %all-reduce.2.cloned.1.call-start = ((), (), s32[]{:S(2)}) async-start(), calls=%async_computation.6 | async-start | bytes 196608 | tf_op jit(solution)/shard_map/psum | solution.py:109
Sparse Core Ops, SparseCore 0:
  12.2 136.2 all-gather.1
  231.3 41.4 all-reduce.1
where the time goes:
time: 284 us; the launch traced here: 282 us
  waiting for transfers between devices  109 us (38%)
  local copies, waits for them, and re-layouts  82.1 us (29%)
  starting transfers between devices  33.1 us (12%)
  matrix products  28.8 us (10%)
  between operations  16.2 us (6%)
  other arithmetic  12.3 us (4%)
    psum x1, waiting for transfers between devices, shards(): summed = lax.psum(owned_sum, 'wafer')  40 us
    all_to_all x1, waiting for transfers between devices, shards(): lax.all_to_all(timestream, 'wafer', split_axis=1, concat_axis=0, tiled=True)  25.7 us
    all_to_all x1, waiting for transfers between devices, shards(): lax.all_to_all(sample_weight, 'wafer', split_axis=1, concat_axis=0, tiled...  20.1 us
    unnamed x19, local copies, waits for them, and re-layouts  12.4 us
    all_to_all x1, starting transfers between devices, shards(): lax.all_to_all(requests, 'tm', split_axis=0, concat_axis=0, tiled=True)  12 us
    all_to_all x1, waiting for transfers between devices, shards(): lax.all_to_all(outgoing, 'tm', split_axis=0, concat_axis=0, tiled=True)  11.3 us
    convert_element_type x2, local copies, waits for them, and re-layouts, shards(): columns.astype(jnp.float32).reshape(det_total, spans_here, samples) - signal  10.7 us
    convert_element_type x2, local copies, waits for them, and re-layouts, shards(): column_weights.astype(jnp.float32).reshape(det_total, spans_here, samples)  10.6 us
  transfers between devices with their start and end apart: 7, of which 6 were waited for; matrix products, arithmetic and copies ran while one was open for 27% of the time, Pallas kernels for 0%

commit v1 on v0

--- a/solution.py
+++ b/solution.py
@@ -106,7 +106,7 @@
         precision=precise_mode,
     )
     owned_sum = owned_sum.reshape(tiles_own, comp_count, pixel_count)
-    summed = lax.psum(owned_sum, "wafer")
+    summed = jnp.sum(lax.all_gather(owned_sum, "wafer"), axis=0)
     residual_next = summed * float(det_total) ** (-0.5)
     direction_next = residual_next + blend_weight * direction
     return (updated, residual_next, direction_next)

time: 284 us -> 255 us (0.90)
  waiting for transfers between devices: 109 us -> 67.4 us
  blocking collectives: 0 us -> 12.6 us
    psum x1 -> x0, waiting for transfers between devices: 40 us -> none  [shards(): summed = lax.psum(owned_sum, 'wafer')]
    all_gather x0 -> x1, blocking collectives: none -> 12.6 us  [shards(): summed = jnp.sum(lax.all_gather(owned_sum, 'wafer'), axis=0)]
  transfers between devices with their start and end apart: 7 -> 6, of which waited for: 6 -> 5; matrix products, arithmetic and copies ran while one was open for 27% -> 30% of each run, Pallas kernels for 0% -> 0%
where the time goes in v1:
time: 255 us; the launch traced here: 253 us
  local copies, waits for them, and re-layouts  82 us (32%)
  waiting for transfers between devices  67.4 us (26%)
  starting transfers between devices  33.3 us (13%)
  matrix products  28.1 us (11%)
  between operations  16.2 us (6%)
  other arithmetic  13 us (5%)
  blocking collectives  12.6 us (5%)
    all_to_all x1, waiting for transfers between devices, shards(): lax.all_to_all(timestream, 'wafer', split_axis=1, concat_axis=0, tiled=True)  25.7 us
    all_to_all x1, waiting for transfers between devices, shards(): lax.all_to_all(sample_weight, 'wafer', split_axis=1, concat_axis=0, tiled...  19.9 us
    all_gather x1, blocking collectives, shards(): summed = jnp.sum(lax.all_gather(owned_sum, 'wafer'), axis=0)  12.6 us
    unnamed x19, local copies, waits for them, and re-layouts  12.3 us
    all_to_all x1, starting transfers between devices, shards(): lax.all_to_all(requests, 'tm', split_axis=0, concat_axis=0, tiled=True)  12 us
    convert_element_type x2, local copies, waits for them, and re-layouts, shards(): columns.astype(jnp.float32).reshape(det_total, spans_here, samples) - signal  10.7 us
    convert_element_type x2, local copies, waits for them, and re-layouts, shards(): column_weights.astype(jnp.float32).reshape(det_total, spans_here, samples)  10.6 us
    convert_element_type x2, local copies, waits for them, and re-layouts, shards(): smoothed.astype(jnp.float32) * column_weights  10.5 us
  transfers between devices with their start and end apart: 6, of which 5 were waited for; matrix products, arithmetic and copies ran while one was open for 30% of the time, Pallas kernels for 0%

profile of v1, /device:TPU:2, one launch (start us, length us, event | category | flops | bytes accessed | tf_op | source)
XLA Modules:
  0.0 252.6 jit_solution(1439315080975928290)
XLA Ops:
  12.9 12.0 %all-to-all-start = ((s32[64,1,2]{2,1,0:T(1,128)}), s32[64,1,2]{2,1,0:T(1,128)S(1)}, u32[]{:S(2)}, u32[]{:S(2)}) async-start(s32[64,1,2]{2,1,0:T(1,128)} %bitcast.2), calls=%async_computation | async-start | bytes 65536 | tf_op jit(solution)/shard_map/all_to_all | solution.py:45
  28.6 4.8 %all-to-all-done = s32[64,1,2]{2,1,0:T(1,128)S(1)} async-done(((s32[64,1,2]{2,1,0:T(1,128)}), s32[64,1,2]{2,1,0:T(1,128)S(1)}, u32[]{:S(2)}, u32[]{:S(2)}) %all-to-all-start) | async-done | bytes 544 | tf_op jit(solution)/shard_map/all_to_all | solution.py:45
  35.9 5.5 %all-to-all-start.2 = ((bf16[64,2,3,256]{3,1,2,0:T(2,128)(2,1)}), bf16[64,2,3,256]{3,1,2,0:T(2,128)(2,1)S(1)}, u32[]{:S(2)}, u32[]{:S(2)}) async-start(bf16[64,2,3,256]{3,1,2,0:T(2,128)(2,1)} %broadcast_select_fusion), calls=%async_computation.2 | async-start | bytes 393216 | tf_op jit(solution)/shard_map/all_to_all | solution.py:48
  45.4 7.2 %all-to-all-done.2 = bf16[64,2,3,256]{3,1,2,0:T(2,128)(2,1)S(1)} async-done(((bf16[64,2,3,256]{3,1,2,0:T(2,128)(2,1)}), bf16[64,2,3,256]{3,1,2,0:T(2,128)(2,1)S(1)}, u32[]{:S(2)}, u32[]{:S(2)}) %all-to-all-start.2) | async-done | bytes 196640 | tf_op jit(solution)/shard_map/all_to_all | solution.py:48
  52.7 4.6 %all-to-all-start.1 = ((bf16[256,4,1024]{0,2,1:T(8,128)(2,1)}), bf16[256,4,1024]{0,2,1:T(8,128)(2,1)}, u32[]{:S(2)}, u32[]{:S(2)}) async-start(bf16[256,4,1024]{0,2,1:T(8,128)(2,1)} %bitcast.102), calls=%async_computation.1 | async-start | bytes 4194304 | tf_op jit(solution)/shard_map/all_to_all | solution.py:63
  61.3 25.7 %all-to-all-done.1 = bf16[256,4,1024]{0,2,1:T(8,128)(2,1)} async-done(((bf16[256,4,1024]{0,2,1:T(8,128)(2,1)}), bf16[256,4,1024]{0,2,1:T(8,128)(2,1)}, u32[]{:S(2)}, u32[]{:S(2)}) %all-to-all-start.1) | async-done | bytes 2097184 | tf_op jit(solution)/shard_map/all_to_all | solution.py:63
  87.1 4.6 %all-to-all-start.3 = ((bf16[256,4,1024]{0,2,1:T(8,128)(2,1)}), bf16[256,4,1024]{0,2,1:T(8,128)(2,1)}, u32[]{:S(2)}, u32[]{:S(2)}) async-start(bf16[256,4,1024]{0,2,1:T(8,128)(2,1)} %bitcast.101), calls=%async_computation.3 | async-start | bytes 4194304 | tf_op jit(solution)/shard_map/all_to_all | solution.py:64
  99.8 4.9 %copy.114 = f32[4,256,1024]{1,0,2:T(4,128)} copy(f32[4,256,1024]{1,2,0:T(8,128)S(1)} %convert_bitcast_fusion.1) | data formatting | bytes 8388608 | tf_op jit(solution)/shard_map/convert_element_type | solution.py:69
  104.8 5.8 %reshape.383 = f32[1024,4,256]{0,2,1:T(8,128)} reshape(f32[4,256,1024]{1,0,2:T(4,128)} %copy.114) | data formatting | bytes 8388608 | tf_op jit(solution)/shard_map/convert_element_type | solution.py:69
  110.6 19.9 %all-to-all-done.3 = bf16[256,4,1024]{0,2,1:T(8,128)(2,1)} async-done(((bf16[256,4,1024]{0,2,1:T(8,128)(2,1)}), bf16[256,4,1024]{0,2,1:T(8,128)(2,1)}, u32[]{:S(2)}, u32[]{:S(2)}) %all-to-all-start.3) | async-done | bytes 2097184 | tf_op jit(solution)/shard_map/all_to_all | solution.py:64
  132.7 4.7 %copy.124 = f32[4,256,1024]{1,0,2:T(4,128)} copy(f32[4,256,1024]{1,2,0:T(8,128)S(1)} %convert_bitcast_fusion) | data formatting | bytes 8388608 | tf_op jit(solution)/shard_map/convert_element_type | solution.py:66
  137.4 5.9 %reshape.384 = f32[1024,4,256]{0,2,1:T(8,128)} reshape(f32[4,256,1024]{1,0,2:T(4,128)} %copy.124) | data formatting | bytes 8388608 | tf_op jit(solution)/shard_map/convert_element_type | solution.py:66
  143.2 7.2 %fusion.2 = bf16[1024,4,256]{0,2,1:T(8,128)(2,1)} fusion(f32[1024,4,256]{0,2,1:T(8,128)} %reshape.384, f32[1024,4,256]{0,2,1:T(8,128)} %reshape.383, f32[4,3,256]{2,1,0:T(4,128)S(1)} %convolution_bitcast_fusion, f32[3,1024]{1,0:T(4,128)S(1)} %copy-done.4), kind=kOutput, calls=%fused_computation.8 | convolution fusion | flops 40894464 | bytes 10510336 | tf_op jit(solution)/shard_map/jd,cjt->dct/dot_general | solution.py:67
  150.4 4.2 %copy.125 = bf16[1024,4,256]{2,1,0:T(4,128)(2,1)} copy(bf16[1024,4,256]{0,2,1:T(8,128)(2,1)} %fusion.2) | data formatting | bytes 4194304 | tf_op jit(solution)/shard_map/convert_element_type | solution.py:71
  162.3 4.4 %reshape.379 = bf16[1024,1024]{1,0:T(8,128)(2,1)} reshape(bf16[4096,256]{1,0:T(8,128)(2,1)} %convolution_convert_fusion.1) | data formatting | bytes 4194304 | tf_op jit(solution)/shard_map/reshape | solution.py:77
  166.7 7.8 %constant_dynamic-slice_fusion = bf16[1,1024,1024]{2,0,1:T(2,128)(2,1)S(1)} fusion(bf16[7,1024,1024]{2,0,1:T(8,128)(2,1)} %all-gather.3.cloned.1.call-done, s32[]{:T(128)S(6)} %select_n.167), kind=kLoop, calls=%fused_computation.81 | loop fusion | bytes 4194308 | tf_op jit(solution)/shard_map/jit(dynamic_index_in_dim)/dynamic_slice | solution.py:59
  178.2 4.3 %reshape.380 = bf16[4096,256]{1,0:T(8,128)(2,1)} reshape(bf16[1024,1024]{1,0:T(8,128)(2,1)} %fusion.6) | data formatting | bytes 4194304 | tf_op jit(solution)/shard_map/reshape | solution.py:80
  182.5 4.3 %fusion = f32[4096,256]{1,0:T(8,128)} fusion(bf16[4096,256]{1,0:T(8,128)(2,1)} %reshape.380, bf16[256,256]{1,0:T(8,128)(2,1)S(1)} %copy-done.2), kind=kOutput, calls=%fused_computation.4 | convolution fusion | flops 538968064 | bytes 6422528 | tf_op jit(solution)/shard_map/dot_general | solution.py:79
  186.8 5.2 %reshape.385 = f32[1024,4,256]{2,1,0:T(4,128)} reshape(f32[4096,256]{1,0:T(8,128)} %fusion) | data formatting | bytes 8388608 | tf_op jit(solution)/shard_map/convert_element_type | solution.py:89
  192.0 5.3 %copy.126 = f32[1024,4,256]{0,2,1:T(8,128)} copy(f32[1024,4,256]{2,1,0:T(4,128)} %reshape.385) | data formatting | bytes 8388608 | tf_op jit(solution)/shard_map/convert_element_type | solution.py:89
  197.2 7.2 %fusion.10 = bf16[4,256,3,1]{1,2,3,0:T(4,128)(2,1)S(1)} fusion(f32[1024,4,256]{0,2,1:T(8,128)} %copy.126, f32[1024,4,256]{0,2,1:T(8,128)} %reshape.384, f32[3,1024]{1,0:T(4,128)S(1)} %copy-done.4), kind=kOutput, calls=%fused_computation.18 | convolution fusion | flops 38800384 | bytes 8407040 | tf_op jit(solution)/shard_map/jd,dct->cjt/dot_general | solution.py:86
  206.4 6.5 %all-to-all-start.4 = ((f32[64,2,3,256]{3,1,2,0:T(2,128)}), f32[64,2,3,256]{3,1,2,0:T(2,128)S(1)}, u32[]{:S(2)}, u32[]{:S(2)}) async-start(f32[64,2,3,256]{3,1,2,0:T(2,128)} %copy.129), calls=%async_computation.4 | async-start | bytes 786432 | tf_op jit(solution)/shard_map/all_to_all | solution.py:99
  218.1 9.7 %all-to-all-done.4 = f32[64,2,3,256]{3,1,2,0:T(2,128)S(1)} async-done(((f32[64,2,3,256]{3,1,2,0:T(2,128)}), f32[64,2,3,256]{3,1,2,0:T(2,128)S(1)}, u32[]{:S(2)}, u32[]{:S(2)}) %all-to-all-start.4) | async-done | bytes 393248 | tf_op jit(solution)/shard_map/all_to_all | solution.py:99
  230.2 12.6 %all-gather = f32[128,3,256]{2,0,1:T(8,128)S(1)} all-gather(f32[32,3,256]{2,0,1:T(8,128)S(1)} %fusion.21), channel_id=2, replica_groups=mesh['tm'=64,'wafer'=4] {'wafer'}, dimensions={0}, use_global_device_ids=true | all-gather | bytes 491520 | tf_op jit(solution)/shard_map/all_gather | solution.py:109
  (70 shorter events, 52.1 us)
Async XLA Ops:
  7.2 89.8 %copy-start = (bf16[4,6,256,256]{3,2,1,0:T(8,128)(2,1)S(1)}, bf16[4,6,256,256]{3,2,1,0:T(8,128)(2,1)}, u32[]{:S(2)}) copy-start(bf16[4,6,256,256]{3,2,1,0:T(8,128)(2,1)} %param.18) | copy-start | bytes 9437188
  7.2 159.5 %all-gather.3.cloned.1.call-start = ((), (), s32[]{:S(2)}) async-start(), calls=%async_computation.5 | async-start | bytes 16842752 | tf_op jit(solution)/shard_map/all_gather | solution.py:60
  12.9 20.6 %all-to-all-start = ((s32[64,1,2]{2,1,0:T(1,128)}), s32[64,1,2]{2,1,0:T(1,128)S(1)}, u32[]{:S(2)}, u32[]{:S(2)}) async-start(s32[64,1,2]{2,1,0:T(1,128)} %bitcast.2), calls=%async_computation | async-start | bytes 65536 | tf_op jit(solution)/shard_map/all_to_all | solution.py:45
  33.5 0.6 copy-start.3
  35.9 16.8 %all-to-all-start.2 = ((bf16[64,2,3,256]{3,1,2,0:T(2,128)(2,1)}), bf16[64,2,3,256]{3,1,2,0:T(2,128)(2,1)S(1)}, u32[]{:S(2)}, u32[]{:S(2)}) async-start(bf16[64,2,3,256]{3,1,2,0:T(2,128)(2,1)} %broadcast_select_fusion), calls=%async_computation.2 | async-start | bytes 393216 | tf_op jit(solution)/shard_map/all_to_all | solution.py:48
  52.7 34.4 %all-to-all-start.1 = ((bf16[256,4,1024]{0,2,1:T(8,128)(2,1)}), bf16[256,4,1024]{0,2,1:T(8,128)(2,1)}, u32[]{:S(2)}, u32[]{:S(2)}) async-start(bf16[256,4,1024]{0,2,1:T(8,128)(2,1)} %bitcast.102), calls=%async_computation.1 | async-start | bytes 4194304 | tf_op jit(solution)/shard_map/all_to_all | solution.py:63
  61.3 30.6 %copy-start.6 = (s32[64]{0:T(128)S(1)}, s32[64]{0:T(128)}, u32[]{:S(2)}) copy-start(s32[64]{0:T(128)} %param.17) | copy-start | bytes 772
  61.3 33.2 %copy-start.5 = (s32[4,6]{1,0:T(4,128)S(1)}, s32[4,6]{1,0:T(4,128)}, u32[]{:S(2)}) copy-start(s32[4,6]{1,0:T(4,128)} %param.19) | copy-start | bytes 292
  87.1 43.4 %all-to-all-start.3 = ((bf16[256,4,1024]{0,2,1:T(8,128)(2,1)}), bf16[256,4,1024]{0,2,1:T(8,128)(2,1)}, u32[]{:S(2)}, u32[]{:S(2)}) async-start(bf16[256,4,1024]{0,2,1:T(8,128)(2,1)} %bitcast.101), calls=%async_computation.3 | async-start | bytes 4194304 | tf_op jit(solution)/shard_map/all_to_all | solution.py:64
  137.4 5.9 %copy-start.4 = (f32[3,1024]{1,0:T(4,128)S(1)}, f32[3,1024]{1,0:T(4,128)}, u32[]{:S(2)}) copy-start(f32[3,1024]{1,0:T(4,128)} %param.14) | copy-start | bytes 36868
  154.6 4.0 %copy-start.2 = (bf16[256,256]{1,0:T(8,128)(2,1)S(1)}, bf16[256,256]{1,0:T(8,128)(2,1)}, u32[]{:S(2)}) copy-start(bf16[256,256]{1,0:T(8,128)(2,1)} %param.15) | copy-start | bytes 393220
  166.7 7.8 %copy-start.1 = (bf16[1024,1024]{1,0:T(8,128)(2,1)S(1)}, bf16[1024,1024]{1,0:T(8,128)(2,1)}, u32[]{:S(2)}) copy-start(bf16[1024,1024]{1,0:T(8,128)(2,1)} %reshape.379) | copy-start | bytes 6291460
  206.4 21.4 %all-to-all-start.4 = ((f32[64,2,3,256]{3,1,2,0:T(2,128)}), f32[64,2,3,256]{3,1,2,0:T(2,128)S(1)}, u32[]{:S(2)}, u32[]{:S(2)}) async-start(f32[64,2,3,256]{3,1,2,0:T(2,128)} %copy.129), calls=%async_computation.4 | async-start | bytes 786432 | tf_op jit(solution)/shard_map/all_to_all | solution.py:99
Sparse Core Ops, SparseCore 0:
  12.2 136.2 all-gather.2
